TPU v7x, 256 devices: a whole 4x4x8 slice. The times are simulated.
256 devices in a mesh: hours: 64 (over z_hi, x, y, core), blocks: 4 (over z_lo).
Axes of the slice: x: 4, y: 4, z: 8 (z_hi: 2, z_lo: 4; z = z_hi * 4 + z_lo), core: 2. Of those that a mesh axis runs over, the one named last changes fastest.
Arguments:
- spectra: float32 [64, 64, 3, 2, 2048], P('hours', 'blocks'), may hold values from -6 to 6
- validity: int32 [64, 64], P('hours', 'blocks'), may hold values from 0 to 1, as said below
Outputs:
- near_stack: float32 [4, 2, 2304, 256], P('blocks', None, 'hours')
- far_stack: float32 [4, 1152, 256], P('blocks', 'hours')
Inputs may be any that keep to these rules, and one draw needn't show every extreme that they name: `validity`: 0 or 1; some stations are invalid in every hour.
All inputs are finite; a program needn't handle non-finite values.
Results may differ from a plain program's by a relative error of at most 0.0058.
Values may be sent and summed in bfloat16 or wider, within the bound.
No kernel may reach another device: no remote copies, remote signals or barrier semaphores. Data moves between devices by JAX's collectives and lax.ppermute only.
A program may use at most 64 MiB of HBM per device.

v0:
```python
import math

import jax
import jax.numpy as jnp
from jax import lax
from jax.sharding import PartitionSpec as P

BAND = 128
LAGS = 256


EPSILON = 1e-06


def passed_along(block, axis, distance):
    devices = range(lax.axis_size(axis))
    route = [((i - distance) % len(devices), i) for i in devices]
    return lax.ppermute(block, axis, route)


def whiten(spectra, validity, band_width):
    hour_count, station_count, comp_count, part_count, freq_count = spectra.shape
    grouped = spectra.reshape(
        hour_count, station_count, comp_count, part_count, freq_count // band_width, band_width
    )
    band_power = jnp.mean(grouped * grouped, axis=(3, 5), keepdims=True)
    valid_f = validity.astype(jnp.float32).reshape(hour_count, station_count, 1, 1, 1, 1)
    scaled = grouped * (valid_f / jnp.sqrt(band_power + EPSILON))
    return scaled.reshape(hour_count, station_count * comp_count, part_count, freq_count).astype(
        jnp.bfloat16
    )


def build_table(freq_count, lag_count):
    freq_index = jnp.arange(freq_count, dtype=jnp.int32)[:, None]
    lag_index = jnp.arange(lag_count, dtype=jnp.int32)[None, :] - lag_count // 2
    residue = freq_index * (lag_index + 2 * freq_count) % (2 * freq_count)
    angles = residue.astype(jnp.float32) * (math.pi / freq_count)
    amplitude = 8.0 / math.sqrt(freq_count)
    return jnp.concatenate([jnp.cos(angles) * amplitude, -jnp.sin(angles) * amplitude], 0).astype(
        jnp.bfloat16
    )


def cross_spectrum(row_block, col_block):
    row_real = row_block[..., :, None, 0, :].astype(jnp.float32)
    row_imag = row_block[..., :, None, 1, :].astype(jnp.float32)
    col_real = col_block[..., None, :, 0, :].astype(jnp.float32)
    col_imag = col_block[..., None, :, 1, :].astype(jnp.float32)
    real_part = row_real * col_real + row_imag * col_imag
    imag_part = row_imag * col_real - row_real * col_imag
    stacked_parts = jnp.stack([real_part, imag_part], -2)
    dims_shape = stacked_parts.shape
    return stacked_parts.reshape(
        dims_shape[:-4] + (dims_shape[-4] * dims_shape[-3], dims_shape[-2] * dims_shape[-1])
    ).astype(jnp.bfloat16)


def expand(counts, comp_count):
    return jnp.repeat(jnp.repeat(counts, comp_count, 0), comp_count, 1).reshape(-1)


def correlate(row_block, col_block, table):
    hour_count, row_count, part_count, freq_count = row_block.shape
    trace_count = col_block.shape[1]
    row_step = 4
    grouped = row_block.reshape(
        hour_count, row_count // row_step, row_step, part_count, freq_count
    ).transpose(1, 0, 2, 3, 4)

    def one_block(sub_rows):
        spectrum = cross_spectrum(sub_rows, col_block)
        return jnp.einsum("hpk,kl->pl", spectrum, table, preferred_element_type=jnp.float32)

    result = lax.map(one_block, grouped)
    return result.reshape(row_count * trace_count, table.shape[1])


def on_device(spectra, validity):
    hour_count, station_count, comp_count, part_count, freq_count = spectra.shape
    trace_count = station_count * comp_count
    half_width = trace_count // 2
    half_stations = station_count // 2
    white = whiten(spectra, validity, BAND)
    table = build_table(freq_count, LAGS)
    valid_wire = validity.astype(jnp.bfloat16)
    block_count = lax.axis_size("blocks")
    near_rounds = block_count // 2
    my_block = lax.axis_index("blocks")
    is_lower = my_block < near_rounds
    panels = [(white, valid_wire)]
    for round_index in range(1, near_rounds + 1):
        panels.append(passed_along((white, valid_wire), "blocks", round_index))
    near_terms = jnp.stack(
        [correlate(white, panels[round_index][0], table) for round_index in range(near_rounds)], 0
    )
    far_white, far_valid = panels[near_rounds]
    far_rows = jnp.where(is_lower, white[:, :half_width], far_white[:, half_width:])
    far_cols = jnp.where(is_lower, far_white, white)
    far_terms = correlate(far_rows, far_cols, table)
    hour_devices = lax.axis_size("hours")
    share_near = trace_count * trace_count // hour_devices
    share_far = half_width * trace_count // hour_devices
    my_slot = lax.axis_index("hours")
    hour_masks = lax.all_gather(validity, "hours", axis=0, tiled=True)
    all_masks = lax.all_gather(hour_masks, "blocks", axis=1, tiled=True).astype(jnp.float32)
    pair_counts = jnp.dot(
        all_masks.T, all_masks, precision=lax.Precision.HIGHEST, preferred_element_type=jnp.float32
    )
    near_sum, far_sum = (
        lax.psum_scatter(near_terms, "hours", scatter_dimension=1, tiled=True),
        lax.psum_scatter(far_terms, "hours", scatter_dimension=0, tiled=True),
    )

    def block_count_of(row_start, row_count, col_start):
        sub_block = lax.dynamic_slice(
            pair_counts, (row_start, col_start), (row_count, station_count)
        )
        return expand(sub_block, comp_count)

    near_full = jnp.stack(
        [
            block_count_of(
                my_block * station_count,
                station_count,
                (my_block - round_index) % block_count * station_count,
            )
            for round_index in range(near_rounds)
        ],
        0,
    )
    far_partner = (my_block + near_rounds) % block_count
    far_full = block_count_of(
        jnp.where(is_lower, my_block * station_count, far_partner * station_count + half_stations),
        half_stations,
        jnp.where(is_lower, far_partner, my_block) * station_count,
    )
    near_count = lax.dynamic_slice_in_dim(near_full, my_slot * share_near, share_near, 1)
    far_count = lax.dynamic_slice_in_dim(far_full, my_slot * share_far, share_far, 0)
    near_stack = near_sum / jnp.maximum(near_count, 1.0)[..., None]
    far_stack = far_sum / jnp.maximum(far_count, 1.0)[..., None]
    return (near_stack[None], far_stack[None])


def solution(mesh):
    in_specs = (P("hours", "blocks", None, None, None), P("hours", "blocks"))
    out_specs = (P("blocks", None, "hours", None), P("blocks", "hours", None))
    return jax.shard_map(
        on_device, mesh=mesh, in_specs=in_specs, out_specs=out_specs, check_vma=False
    )
```

profile of v0, /device:TPU:1, one launch (start us, length us, event | category | flops | bytes accessed | tf_op | source)
XLA Modules:
  0.0 1250.7 jit_solution(14213586231234972083)
XLA Ops:
  11.8 3.8 collective-permute-start.1
  18.1 8.7 multiply_convert_fusion.1
  29.7 141.1 %while.30 = (s32[]{:T(128)}, f32[12,192,256]{2,1,0:T(8,128)S(1)}, bf16[12,1,4,2,2048]{4,3,2,1,0:T(2,128)(2,1)}, bf16[1,48,2,2048]{3,2,1,0:T(2,128)(2,1)}, bf16[4096,256]{1,0:T(8,128)(2,1)}, /*index=5*/s32[]{:T(128)}) while((s32[]{:T(128)}, f32[12,192,256]{2,1,0:T(8,128)S(1)}, bf16[12,1,4,2,2048]{4,3,2,1,0:T(2,128)(2,1)}, ...), condition=%wide.region_3.4_spmd, body=%wide.region_2.3_spmd.sunk | while | flops 409157632 | bytes 24019048 | solution.py:75
  35.9 3.3 pad_maximum_fusion.8
  44.4 3.3 add_convert_fusion.6
  47.7 3.3 pad_maximum_fusion.8
  56.1 3.3 add_convert_fusion.6
  59.5 3.3 pad_maximum_fusion.8
  67.9 3.3 add_convert_fusion.6
  71.2 3.3 pad_maximum_fusion.8
  83.0 3.3 pad_maximum_fusion.8
  94.7 3.3 pad_maximum_fusion.8
  106.5 3.3 pad_maximum_fusion.8
  118.3 3.3 pad_maximum_fusion.8
  130.0 3.3 pad_maximum_fusion.8
  141.8 3.3 pad_maximum_fusion.8
  153.6 3.3 pad_maximum_fusion.8
  165.3 3.3 pad_maximum_fusion.8
  170.8 120.6 %all-gather = s32[64,1,16]{2,1,0:T(1,128)} all-gather(s32[1,1,16]{2,1,0:T(1,128)S(1)} %bitcast.142), channel_id=1, replica_groups=mesh['hours'=64,'blocks'=4] {'hours'}, dimensions={0}, use_global_device_ids=true | all-gather | bytes 4160 | tf_op jit(solution)/shard_map/all_gather | solution.py:105
  292.2 3.4 stack_reshape.6
  295.7 10.9 all_gather.7
  306.8 126.4 %while.31 = (s32[]{:T(128)}, f32[12,192,256]{2,1,0:T(8,128)S(1)}, bf16[12,1,4,2,2048]{4,3,2,1,0:T(2,128)(2,1)}, bf16[1,48,2,2048]{3,2,1,0:T(2,128)(2,1)S(1)}, bf16[4096,256]{1,0:T(8,128)(2,1)}, /*index=5*/s32[]{:T(128)}) while((s32[]{:T(128)}, f32[12,192,256]{2,1,0:T(8,128)S(1)}, bf16[12,1,4,2,2048]{4,3,2,1,0:T(2,128)(2,1)}, ...), condition=%wide.region_5.6_spmd, body=%wide.region_4.5_spmd.sunk | while | flops 409157632 | bytes 24019048 | solution.py:75
  312.0 3.3 pad_maximum_fusion.9
  322.5 3.3 pad_maximum_fusion.9
  333.0 3.3 pad_maximum_fusion.9
  343.5 3.3 pad_maximum_fusion.9
  354.1 3.3 pad_maximum_fusion.9
  364.6 3.3 pad_maximum_fusion.9
  375.1 3.3 pad_maximum_fusion.9
  385.6 3.3 pad_maximum_fusion.9
  396.1 3.3 pad_maximum_fusion.9
  406.6 3.3 pad_maximum_fusion.9
  417.2 3.3 pad_maximum_fusion.9
  427.7 3.3 pad_maximum_fusion.9
  433.2 3.5 stack_reshape.7
  436.7 7.7 pad_maximum_fusion.3
  447.4 58.6 %while.32 = (s32[]{:T(128)}, f32[6,192,256]{2,1,0:T(8,128)S(1)}, bf16[6,1,4,2,2048]{4,3,2,1,0:T(2,128)(2,1)S(1)}, bf16[1,48,2,2048]{3,2,1,0:T(2,128)(2,1)S(1)}, bf16[4096,256]{1,0:T(8,128)(2,1)}, /*index=5*/s32[]{:T(128)}) while((s32[]{:T(128)}, f32[6,192,256]{2,1,0:T(8,128)S(1)}, bf16[6,1,4,2,2048]{4,3,2,1,0:T(2,128)(2,1)S(1)}, ...), condition=%wide.region_8.9_spmd, body=%wide.region_7.8_spmd.sunk | while | flops 409157632 | bytes 24019048 | solution.py:75
  451.6 3.3 pad_maximum_fusion.10
  461.4 3.3 pad_maximum_fusion.10
  471.2 3.3 pad_maximum_fusion.10
  480.9 3.3 pad_maximum_fusion.10
  490.7 3.3 pad_maximum_fusion.10
  500.5 3.3 pad_maximum_fusion.10
  506.0 213.0 %fusion = f32[24,256]{1,0:T(8,128)S(1)} fusion(f32[1152,256]{1,0:T(8,128)S(1)} %bitcast.139), kind=kCustom, calls=%all-reduce-scatter | all-reduce-scatter fusion | flops 393217 | bytes 1205248
  724.6 10.9 collective-permute-start.13
  753.6 4.3 collective-permute-start.6
  762.1 4.1 collective-permute-start.9
  771.2 471.0 %all-reduce.5.cloned.1.call-done = f32[2,2304,256]{2,0,1:T(2,128)} async-done(((f32[2,2304,256]{2,0,1:T(2,128)}), f32[2,2304,256]{2,0,1:T(2,128)}) %all-reduce.5.cloned.1.call-update) | async-done | bytes 4718608
  (390 shorter events, 260.5 us)
Async XLA Ops:
  7.2 2.6 copy-start.10
  7.2 1235.1 %all-reduce.5.cloned.1.call-start = ((), (), s32[]{:S(2)}) async-start(), calls=%async_computation | async-start | bytes 9437184
  11.8 432.6 %collective-permute-start.1 = (bf16[1,48,2,2048]{3,2,1,0:T(2,128)(2,1)}, bf16[1,48,2,2048]{3,2,1,0:T(2,128)(2,1)}, u32[]{:S(2)}, u32[]{:S(2)}) collective-permute-start(bf16[1,48,2,2048]{3,2,1,0:T(2,128)(2,1)} %multiply_convert_fusion.2), channel_id=1, source_target_pairs={{2,0},{3,1},{0,2},{1,3},{6,4},{7,5},{4,6},{5,7},{10,8},{11,9},{8,1... | collective-permute-start | bytes 1179656 | tf_op jit(solution)/shard_map/ppermute | solution.py:18
  15.6 291.0 %collective-permute-start = (bf16[1,48,2,2048]{3,2,1,0:T(2,128)(2,1)}, bf16[1,48,2,2048]{3,2,1,0:T(2,128)(2,1)S(1)}, u32[]{:S(2)}, u32[]{:S(2)}) collective-permute-start(bf16[1,48,2,2048]{3,2,1,0:T(2,128)(2,1)} %multiply_convert_fusion.2), channel_id=1, source_target_pairs={{3,0},{0,1},{1,2},{2,3},{7,4},{4,5},{5,6},{6,7},{11,8},{8,9},{9,10... | collective-permute-start | bytes 1179656 | tf_op jit(solution)/shard_map/ppermute | solution.py:18
  39.3 1.6 copy-start.3
  51.0 1.6 copy-start.3
  62.8 1.6 copy-start.3
  74.5 1.6 copy-start.3
  86.3 1.6 copy-start.3
  98.1 1.6 copy-start.3
  109.8 1.6 copy-start.3
  121.6 1.6 copy-start.3
  133.4 1.6 copy-start.3
  145.1 1.6 copy-start.3
  156.9 1.6 copy-start.3
  168.6 1.6 copy-start.3
  315.3 1.6 copy-start.4
  325.8 1.6 copy-start.4
  336.3 1.6 copy-start.4
  346.9 1.6 copy-start.4
  357.4 1.6 copy-start.4
  367.9 1.6 copy-start.4
  378.4 1.6 copy-start.4
  388.9 1.6 copy-start.4
  399.5 1.6 copy-start.4
  420.5 1.6 copy-start.4
  444.4 2.9 copy-start.7
  447.3 273.0 %copy-start.8 = (s32[64,64]{0,1:T(8,128)S(1)}, s32[64,64]{0,1:T(8,128)}, u32[]{:S(2)}) copy-start(s32[64,64]{0,1:T(8,128)} %all_gather.7) | copy-start | bytes 49156
  454.9 1.6 copy-start.5
  464.7 1.6 copy-start.5
  503.8 1.6 copy-start.5
  719.0 47.3 %copy-start.9 = (u32[256]{0:T(256)S(1)}, u32[256]{0:T(256)}, u32[]{:S(2)}) copy-start(u32[256]{0:T(256)} %constant.117) | copy-start | bytes 3076
  719.1 16.5 %collective-permute-start.17 = (f32[18,256]{1,0:T(8,128)S(1)}, f32[18,256]{1,0:T(8,128)S(1)}, u32[]{:S(2)}, u32[]{:S(2)}) collective-permute-start(f32[18,256]{1,0:T(8,128)S(1)} %slice.52), channel_id=1, source_target_pairs={{0,64},{4,68},{8,72},{12,76},{16,80},{20,84},{24,88},{28,92},{32,9... | collective-permute-start | bytes 55304
  720.6 18.0 %collective-permute-start.10 = (f32[24,256]{1,0:T(8,128)S(1)}, f32[24,256]{1,0:T(8,128)S(1)}, u32[]{:S(2)}, u32[]{:S(2)}) collective-permute-start(f32[24,256]{1,0:T(8,128)S(1)} %fusion), channel_id=1, source_target_pairs={{0,36},{4,40},{8,44},{12,48},{16,52},{20,56},{24,60},{28,64},{32,6... | collective-permute-start | bytes 73736
  721.9 18.3 %collective-permute-start.11 = (f32[24,256]{1,0:T(8,128)S(1)}, f32[24,256]{1,0:T(8,128)S(1)}, u32[]{:S(2)}, u32[]{:S(2)}) collective-permute-start(f32[24,256]{1,0:T(8,128)S(1)} %fusion), channel_id=1, source_target_pairs={{0,40},{4,44},{8,48},{12,52},{16,56},{20,60},{24,64},{28,68},{32,7... | collective-permute-start | bytes 73736
  723.2 19.0 %collective-permute-start.12 = (f32[24,256]{1,0:T(8,128)S(1)}, f32[24,256]{1,0:T(8,128)S(1)}, u32[]{:S(2)}, u32[]{:S(2)}) collective-permute-start(f32[24,256]{1,0:T(8,128)S(1)} %fusion), channel_id=1, source_target_pairs={{0,44},{4,48},{8,52},{12,56},{16,60},{20,64},{24,68},{28,72},{32,7... | collective-permute-start | bytes 73736
  724.6 20.7 %collective-permute-start.13 = (f32[24,256]{1,0:T(8,128)S(1)}, f32[24,256]{1,0:T(8,128)S(1)}, u32[]{:S(2)}, u32[]{:S(2)}) collective-permute-start(f32[24,256]{1,0:T(8,128)S(1)} %fusion), channel_id=1, source_target_pairs={{0,48},{4,52},{8,56},{12,60},{16,64},{20,68},{24,72},{28,76},{32,8... | collective-permute-start | bytes 73736
  735.5 12.8 %collective-permute-start.14 = (f32[24,256]{1,0:T(8,128)S(1)}, f32[24,256]{1,0:T(8,128)S(1)}, u32[]{:S(2)}, u32[]{:S(2)}) collective-permute-start(f32[24,256]{1,0:T(8,128)S(1)} %fusion), channel_id=1, source_target_pairs={{0,52},{4,56},{8,60},{12,64},{16,68},{20,72},{24,76},{28,80},{32,8... | collective-permute-start | bytes 73736
  738.6 12.6 %collective-permute-start.15 = (f32[24,256]{1,0:T(8,128)S(1)}, f32[24,256]{1,0:T(8,128)S(1)}, u32[]{:S(2)}, u32[]{:S(2)}) collective-permute-start(f32[24,256]{1,0:T(8,128)S(1)} %fusion), channel_id=1, source_target_pairs={{0,56},{4,60},{8,64},{12,68},{16,72},{20,76},{24,80},{28,84},{32,8... | collective-permute-start | bytes 73736
  740.3 13.4 %collective-permute-start.16 = (f32[24,256]{1,0:T(8,128)S(1)}, f32[24,256]{1,0:T(8,128)S(1)}, u32[]{:S(2)}, u32[]{:S(2)}) collective-permute-start(f32[24,256]{1,0:T(8,128)S(1)} %fusion), channel_id=1, source_target_pairs={{0,60},{4,64},{8,68},{12,72},{16,76},{20,80},{24,84},{28,88},{32,9... | collective-permute-start | bytes 73736
  742.2 15.8 %collective-permute-start.2 = (f32[24,256]{1,0:T(8,128)S(1)}, f32[24,256]{1,0:T(8,128)S(1)}, u32[]{:S(2)}, u32[]{:S(2)}) collective-permute-start(f32[24,256]{1,0:T(8,128)S(1)} %fusion), channel_id=1, source_target_pairs={{0,4},{4,8},{8,12},{12,16},{16,20},{20,24},{24,28},{28,32},{32,36}... | collective-permute-start | bytes 73736
  745.3 15.5 %collective-permute-start.3 = (f32[24,256]{1,0:T(8,128)S(1)}, f32[24,256]{1,0:T(8,128)S(1)}, u32[]{:S(2)}, u32[]{:S(2)}) collective-permute-start(f32[24,256]{1,0:T(8,128)S(1)} %fusion), channel_id=1, source_target_pairs={{0,8},{4,12},{8,16},{12,20},{16,24},{20,28},{24,32},{28,36},{32,40... | collective-permute-start | bytes 73736
  748.4 13.7 %collective-permute-start.4 = (f32[24,256]{1,0:T(8,128)S(1)}, f32[24,256]{1,0:T(8,128)S(1)}, u32[]{:S(2)}, u32[]{:S(2)}) collective-permute-start(f32[24,256]{1,0:T(8,128)S(1)} %fusion), channel_id=1, source_target_pairs={{0,12},{4,16},{8,20},{12,24},{16,28},{20,32},{24,36},{28,40},{32,4... | collective-permute-start | bytes 73736
  751.2 17.1 %collective-permute-start.5 = (f32[24,256]{1,0:T(8,128)S(1)}, f32[24,256]{1,0:T(8,128)S(1)}, u32[]{:S(2)}, u32[]{:S(2)}) collective-permute-start(f32[24,256]{1,0:T(8,128)S(1)} %fusion), channel_id=1, source_target_pairs={{0,16},{4,20},{8,24},{12,28},{16,32},{20,36},{24,40},{28,44},{32,4... | collective-permute-start | bytes 73736
  753.6 14.7 %collective-permute-start.6 = (f32[24,256]{1,0:T(8,128)S(1)}, f32[24,256]{1,0:T(8,128)S(1)}, u32[]{:S(2)}, u32[]{:S(2)}) collective-permute-start(f32[24,256]{1,0:T(8,128)S(1)} %fusion), channel_id=1, source_target_pairs={{0,20},{4,24},{8,28},{12,32},{16,36},{20,40},{24,44},{28,48},{32,5... | collective-permute-start | bytes 73736
  757.9 10.4 collective-permute-start.7
  760.8 7.5 collective-permute-start.8
  762.1 6.2 collective-permute-start.9
  (9 other events, 13.3 us)
Sparse Core Ops, SparseCore 0:
  444.5 797.6 all-reduce.4
where the time goes:
time: 1250 us
  waiting for transfers between devices  471 us (38%)
  blocking collectives  345 us (28%)
  other arithmetic  259 us (21%)
  local copies, waits for them, and re-layouts  89.5 us (7%)
  starting transfers between devices  50.6 us (4%)
  matrix products  17.5 us (1%)
  between operations  15.9 us (1%)
    unnamed x18, waiting for transfers between devices  471 us
    unnamed x1, blocking collectives  213 us
    all_gather x1, blocking collectives, on_device(): hour_masks = lax.all_gather(validity, 'hours', axis=0, tiled=True)  121 us
    another operation x31, other arithmetic  108 us
    another operation x30, other arithmetic, cross_spectrum(): stacked_parts = jnp.stack([real_part, imag_part], -2)  99.6 us
    while x150, local copies, waits for them, and re-layouts  55.7 us
    unnamed x17, starting transfers between devices  45.1 us
    convert_element_type x30, other arithmetic, cross_spectrum(): col_real = col_block[..., None, :, 0, :].astype(jnp.float32)  31.3 us
  transfers between devices with their start and end apart: 19, of which 1 were waited for; matrix products, arithmetic and copies ran while one was open for 44% of the time, Pallas kernels for 0%

commit v1 on v0

--- a/solution.py
+++ b/solution.py
@@ -80,7 +80,6 @@
     hour_count, station_count, comp_count, part_count, freq_count = spectra.shape
     trace_count = station_count * comp_count
     half_width = trace_count // 2
-    half_stations = station_count // 2
     white = whiten(spectra, validity, BAND)
     table = build_table(freq_count, LAGS)
     valid_wire = validity.astype(jnp.bfloat16)
@@ -98,47 +97,47 @@
     far_rows = jnp.where(is_lower, white[:, :half_width], far_white[:, half_width:])
     far_cols = jnp.where(is_lower, far_white, white)
     far_terms = correlate(far_rows, far_cols, table)
-    hour_devices = lax.axis_size("hours")
-    share_near = trace_count * trace_count // hour_devices
-    share_far = half_width * trace_count // hour_devices
-    my_slot = lax.axis_index("hours")
-    hour_masks = lax.all_gather(validity, "hours", axis=0, tiled=True)
-    all_masks = lax.all_gather(hour_masks, "blocks", axis=1, tiled=True).astype(jnp.float32)
-    pair_counts = jnp.dot(
-        all_masks.T, all_masks, precision=lax.Precision.HIGHEST, preferred_element_type=jnp.float32
-    )
-    near_sum, far_sum = (
-        lax.psum_scatter(near_terms, "hours", scatter_dimension=1, tiled=True),
-        lax.psum_scatter(far_terms, "hours", scatter_dimension=0, tiled=True),
-    )
 
-    def block_count_of(row_start, row_count, col_start):
-        sub_block = lax.dynamic_slice(
-            pair_counts, (row_start, col_start), (row_count, station_count)
-        )
-        return expand(sub_block, comp_count)
+    def trace_valid(valid):
+        return jnp.repeat(valid.reshape(-1).astype(jnp.float32), comp_count)
 
-    near_full = jnp.stack(
+    own_valid = trace_valid(valid_wire)
+    near_pairs = jnp.stack(
         [
-            block_count_of(
-                my_block * station_count,
-                station_count,
-                (my_block - round_index) % block_count * station_count,
-            )
+            (own_valid[:, None] * trace_valid(panels[round_index][1])[None, :]).reshape(-1)
             for round_index in range(near_rounds)
         ],
         0,
     )
-    far_partner = (my_block + near_rounds) % block_count
-    far_full = block_count_of(
-        jnp.where(is_lower, my_block * station_count, far_partner * station_count + half_stations),
-        half_stations,
-        jnp.where(is_lower, far_partner, my_block) * station_count,
+    far_trace_valid = trace_valid(far_valid)
+    far_row_valid = jnp.where(is_lower, own_valid[:half_width], far_trace_valid[half_width:])
+    far_col_valid = jnp.where(is_lower, far_trace_valid, own_valid)
+    far_pairs = (far_row_valid[:, None] * far_col_valid[None, :]).reshape(-1)
+
+    hour_devices = lax.axis_size("hours")
+    share_near = trace_count * trace_count // hour_devices
+    share_far = half_width * trace_count // hour_devices
+    lag_count = table.shape[1]
+    near_slots = near_terms.reshape(near_rounds, hour_devices, share_near, lag_count).transpose(1, 0, 2, 3)
+    far_slots = far_terms.reshape(hour_devices, share_far, lag_count)
+    count_slots = jnp.concatenate(
+        [
+            near_pairs.reshape(near_rounds, hour_devices, share_near).transpose(1, 0, 2).reshape(hour_devices, -1),
+            far_pairs.reshape(hour_devices, share_far),
+        ],
+        1,
     )
-    near_count = lax.dynamic_slice_in_dim(near_full, my_slot * share_near, share_near, 1)
-    far_count = lax.dynamic_slice_in_dim(far_full, my_slot * share_far, share_far, 0)
-    near_stack = near_sum / jnp.maximum(near_count, 1.0)[..., None]
-    far_stack = far_sum / jnp.maximum(far_count, 1.0)[..., None]
+    row_count = near_rounds * share_near + share_far
+    count_row = jnp.pad(count_slots, ((0, 0), (0, lag_count - row_count)))[:, None, :]
+    outgoing = jnp.concatenate(
+        [near_slots.reshape(hour_devices, near_rounds * share_near, lag_count), far_slots, count_row], 1
+    )
+    incoming = lax.all_to_all(outgoing, "hours", 0, 0, tiled=True)
+    total = jnp.sum(incoming, axis=0)
+    pair_counts = jnp.maximum(total[row_count, :row_count], 1.0)
+    stacked = total[:row_count] / pair_counts[:, None]
+    near_stack = stacked[: near_rounds * share_near].reshape(near_rounds, share_near, lag_count)
+    far_stack = stacked[near_rounds * share_near :]
     return (near_stack[None], far_stack[None])
 
 

time: 1250 us -> 537 us (0.43)
  waiting for transfers between devices: 471 us -> 0.02 us
  blocking collectives: 345 us -> 156 us
  starting transfers between devices: 50.6 us -> 7.36 us
  between operations: 15.9 us -> 0.92 us
    unnamed x18 -> x0, waiting for transfers between devices: 471 us -> none
    unnamed x1 -> x0, blocking collectives: 213 us -> none
    all_to_all x0 -> x1, blocking collectives: none -> 156 us  [on_device(): incoming = lax.all_to_all(outgoing, 'hours', 0, 0, tiled=True)]
    all_gather x2 -> x0, blocking collectives: 131 us -> none  [the longest x1 121 us: on_device(): hour_masks = lax.all_gather(validity, 'hours', axis=0, tiled=True)]
    unnamed x17 -> x0, starting transfers between devices: 45.1 us -> none
    another operation x32 -> x31, other arithmetic: 115 us -> 108 us
  transfers between devices with their start and end apart: 19 -> 4, of which waited for: 1 -> 0; matrix products, arithmetic and copies ran while one was open for 44% -> 39% of each run, Pallas kernels for 0% -> 0%
where the time goes in v1:
time: 537 us; the launch traced here: 534 us
  other arithmetic  258 us (48%)
  blocking collectives  156 us (29%)
  local copies, waits for them, and re-layouts  92.2 us (17%)
  matrix products  17.3 us (3%)
  starting transfers between devices  7.36 us (1%)
    all_to_all x1, blocking collectives, on_device(): incoming = lax.all_to_all(outgoing, 'hours', 0, 0, tiled=True)  156 us
    another operation x31, other arithmetic  108 us
    another operation x30, other arithmetic, cross_spectrum(): stacked_parts = jnp.stack([real_part, imag_part], -2)  99.6 us
    while x150, local copies, waits for them, and re-layouts  55.7 us
    convert_element_type x30, other arithmetic, cross_spectrum(): col_real = col_block[..., None, :, 0, :].astype(jnp.float32)  31.7 us
    squeeze x30, local copies, waits for them, and re-layouts, correlate(): result = lax.map(one_block, grouped)  19.1 us
    dot_general x30, matrix products, one_block(): jnp.einsum('hpk,kl->pl', spectrum, table, preferred_element_type=jnp.floa...  17.3 us
  transfers between devices with their start and end apart: 4, of which 0 were waited for; matrix products, arithmetic and copies ran while one was open for 39% of the time, Pallas kernels for 0%

profile of v1, /device:TPU:1, one launch (start us, length us, event | category | flops | bytes accessed | tf_op | source)
XLA Modules:
  0.0 533.9 jit_solution(3846955530141173705)
XLA Ops:
  1.4 3.8 collective-permute-start.3
  14.2 8.7 %multiply_convert_fusion.1 = (bf16[2048,256]{1,0:T(8,128)(2,1)S(1)}, bf16[2048,256]{1,0:T(8,128)(2,1)S(1)}) fusion(s32[256]{0:T(256)S(1)} %iota_add_fusion), kind=kLoop, calls=%fused_computation.52 | loop fusion | flops 9961472 | bytes 2098176 | tf_op jit(solution)/shard_map/convert.19
  26.0 141.6 %while.30 = (s32[]{:T(128)}, f32[12,192,256]{2,1,0:T(8,128)S(1)}, bf16[12,1,4,2,2048]{4,3,2,1,0:T(2,128)(2,1)}, bf16[1,48,2,2048]{3,2,1,0:T(2,128)(2,1)}, bf16[4096,256]{1,0:T(8,128)(2,1)}, /*index=5*/s32[]{:T(128)}) while((s32[]{:T(128)}, f32[12,192,256]{2,1,0:T(8,128)S(1)}, bf16[12,1,4,2,2048]{4,3,2,1,0:T(2,128)(2,1)}, ...), condition=%wide.region_3.4_spmd, body=%wide.region_2.3_spmd.sunk | while | flops 409157632 | bytes 24019048 | solution.py:75
  32.3 3.3 pad_maximum_fusion.8
  40.8 3.3 add_convert_fusion.6
  44.1 3.3 pad_maximum_fusion.8
  55.9 3.3 pad_maximum_fusion.8
  64.4 3.3 add_convert_fusion.6
  67.7 3.3 pad_maximum_fusion.8
  76.2 3.3 add_convert_fusion.6
  79.5 3.3 pad_maximum_fusion.8
  88.0 3.3 add_convert_fusion.6
  91.3 3.3 pad_maximum_fusion.8
  99.8 3.3 add_convert_fusion.6
  103.1 3.3 pad_maximum_fusion.8
  114.9 3.3 pad_maximum_fusion.8
  123.4 3.3 add_convert_fusion.6
  126.7 3.3 pad_maximum_fusion.8
  138.5 3.3 pad_maximum_fusion.8
  147.0 3.3 add_convert_fusion.6
  150.3 3.3 pad_maximum_fusion.8
  162.1 3.3 pad_maximum_fusion.8
  174.1 58.8 %while.32 = (s32[]{:T(128)}, f32[6,192,256]{2,1,0:T(8,128)S(1)}, bf16[6,1,4,2,2048]{4,3,2,1,0:T(2,128)(2,1)S(1)}, bf16[1,48,2,2048]{3,2,1,0:T(2,128)(2,1)S(1)}, bf16[4096,256]{1,0:T(8,128)(2,1)}, /*index=5*/s32[]{:T(128)}) while((s32[]{:T(128)}, f32[6,192,256]{2,1,0:T(8,128)S(1)}, bf16[6,1,4,2,2048]{4,3,2,1,0:T(2,128)(2,1)S(1)}, ...), condition=%wide.region_7.8_spmd, body=%wide.region_6.7_spmd.sunk | while | flops 409157632 | bytes 24019048 | solution.py:75
  175.2 3.3 add_convert_fusion.8
  178.5 3.3 pad_maximum_fusion.10
  185.0 3.3 add_convert_fusion.8
  188.3 3.3 pad_maximum_fusion.10
  194.8 3.3 add_convert_fusion.8
  198.1 3.3 pad_maximum_fusion.10
  207.8 3.3 pad_maximum_fusion.10
  217.6 3.3 pad_maximum_fusion.10
  227.4 3.3 pad_maximum_fusion.10
  234.7 126.2 %while.31 = (s32[]{:T(128)}, f32[12,192,256]{2,1,0:T(8,128)S(1)}, bf16[12,1,4,2,2048]{4,3,2,1,0:T(2,128)(2,1)}, bf16[1,48,2,2048]{3,2,1,0:T(2,128)(2,1)S(1)}, bf16[4096,256]{1,0:T(8,128)(2,1)}, /*index=5*/s32[]{:T(128)}) while((s32[]{:T(128)}, f32[12,192,256]{2,1,0:T(8,128)S(1)}, bf16[12,1,4,2,2048]{4,3,2,1,0:T(2,128)(2,1)}, ...), condition=%wide.region_5.6_spmd, body=%wide.region_4.5_spmd.sunk | while | flops 409157632 | bytes 24019048 | solution.py:75
  239.7 3.3 pad_maximum_fusion.9
  250.2 3.3 pad_maximum_fusion.9
  260.7 3.3 pad_maximum_fusion.9
  271.3 3.3 pad_maximum_fusion.9
  281.8 3.3 pad_maximum_fusion.9
  292.3 3.3 pad_maximum_fusion.9
  302.8 3.3 pad_maximum_fusion.9
  313.3 3.3 pad_maximum_fusion.9
  323.8 3.3 pad_maximum_fusion.9
  334.4 3.3 pad_maximum_fusion.9
  344.9 3.3 pad_maximum_fusion.9
  355.4 3.3 pad_maximum_fusion.9
  362.3 3.5 stack.29
  370.1 3.5 copy.15
  373.6 155.7 %all_to_all.5 = f32[64,91,256]{2,1,0:T(8,128)} all-to-all(f32[64,91,256]{2,1,0:T(8,128)S(1)} %copy.15), channel_id=1, replica_groups=mesh['hours'=64,'blocks'=4] {'hours'}, dimensions={0} | all-to-all | bytes 11927552 | tf_op jit(solution)/shard_map/all_to_all | solution.py:135
  (366 shorter events, 222.4 us)
Async XLA Ops:
  1.4 167.9 %collective-permute-start.3 = (bf16[1,16]{1,0:T(2,128)(2,1)S(1)}, bf16[1,16]{1,0:T(2,128)(2,1)}, u32[]{:S(2)}, u32[]{:S(2)}) collective-permute-start(bf16[1,16]{1,0:T(2,128)(2,1)S(1)} %get-tuple-element.155), channel_id=1, source_target_pairs={{2,0},{3,1},{0,2},{1,3},{6,4},{7,5},{4,6},{5,7},{10,8},{11,9},{8,1... | collective-permute-start | bytes 104 | tf_op jit(solution)/shard_map/ppermute | solution.py:18
  5.2 165.4 %collective-permute-start.2 = (bf16[1,16]{1,0:T(2,128)(2,1)S(1)}, bf16[1,16]{1,0:T(2,128)(2,1)S(1)}, u32[]{:S(2)}, u32[]{:S(2)}) collective-permute-start(bf16[1,16]{1,0:T(2,128)(2,1)S(1)} %get-tuple-element.155), channel_id=1, source_target_pairs={{3,0},{0,1},{1,2},{2,3},{7,4},{4,5},{5,6},{6,7},{11,8},{8,9},{9,10... | collective-permute-start | bytes 104 | tf_op jit(solution)/shard_map/ppermute | solution.py:18
  9.1 1.1 copy-start
  10.0 1.4 copy-start.4
  11.4 159.8 %collective-permute-start.1 = (bf16[1,48,2,2048]{3,2,1,0:T(2,128)(2,1)}, bf16[1,48,2,2048]{3,2,1,0:T(2,128)(2,1)}, u32[]{:S(2)}, u32[]{:S(2)}) collective-permute-start(bf16[1,48,2,2048]{3,2,1,0:T(2,128)(2,1)} %multiply_convert_fusion.2), channel_id=1, source_target_pairs={{2,0},{3,1},{0,2},{1,3},{6,4},{7,5},{4,6},{5,7},{10,8},{11,9},{8,1... | collective-permute-start | bytes 1179656 | tf_op jit(solution)/shard_map/ppermute | solution.py:18
  11.4 223.1 %collective-permute-start = (bf16[1,48,2,2048]{3,2,1,0:T(2,128)(2,1)}, bf16[1,48,2,2048]{3,2,1,0:T(2,128)(2,1)S(1)}, u32[]{:S(2)}, u32[]{:S(2)}) collective-permute-start(bf16[1,48,2,2048]{3,2,1,0:T(2,128)(2,1)} %multiply_convert_fusion.2), channel_id=1, source_target_pairs={{3,0},{0,1},{1,2},{2,3},{7,4},{4,5},{5,6},{6,7},{11,8},{8,9},{9,10... | collective-permute-start | bytes 1179656 | tf_op jit(solution)/shard_map/ppermute | solution.py:18
  23.0 1.5 copy-start.9
  35.6 1.6 copy-start.6
  47.4 1.6 copy-start.6
  59.2 1.6 copy-start.6
  71.0 1.6 copy-start.6
  82.8 1.6 copy-start.6
  94.6 1.6 copy-start.6
  106.4 1.6 copy-start.6
  118.2 1.6 copy-start.6
  130.0 1.6 copy-start.6
  141.8 1.6 copy-start.6
  153.6 1.6 copy-start.6
  165.4 1.6 copy-start.6
  169.3 3.2 copy-start.5
  170.8 3.2 copy-start.10
  181.9 1.6 copy-start.7
  191.6 1.6 copy-start.7
  201.4 1.6 copy-start.7
  211.2 1.6 copy-start.7
  220.9 1.6 copy-start.7
  230.7 1.6 copy-start.7
  243.0 1.6 copy-start.8
  253.6 1.6 copy-start.8
  264.1 1.6 copy-start.8
  274.6 1.6 copy-start.8
  285.1 1.6 copy-start.8
  295.6 1.6 copy-start.8
  306.1 1.6 copy-start.8
  316.7 1.6 copy-start.8
  327.2 1.6 copy-start.8
  337.7 1.6 copy-start.8
  348.2 1.6 copy-start.8
  358.7 1.6 copy-start.8
  360.9 1.4 copy-start.2
  362.3 3.5 copy-start.1
  367.9 1.4 copy-start.3

commit v2 on v1

--- a/solution.py
+++ b/solution.py
@@ -3,6 +3,8 @@
 import jax
 import jax.numpy as jnp
 from jax import lax
+from jax.experimental import pallas as pl
+from jax.experimental.pallas import tpu as pltpu
 from jax.sharding import PartitionSpec as P
 
 BAND = 128
@@ -60,20 +62,47 @@
     return jnp.repeat(jnp.repeat(counts, comp_count, 0), comp_count, 1).reshape(-1)
 
 
+def correlate_kernel(rows_ref, cols_ref, table_ref, out_ref, cross_ref):
+    row_step = rows_ref.shape[0]
+    col_count, wide = cols_ref.shape
+    freq_count = wide // 2
+    chunk = 256
+    for start in range(0, freq_count, chunk):
+        col_real = cols_ref[:, start : start + chunk]
+        col_imag = cols_ref[:, freq_count + start : freq_count + start + chunk]
+        for row in range(row_step):
+            row_real = rows_ref[row : row + 1, start : start + chunk]
+            row_imag = rows_ref[row : row + 1, freq_count + start : freq_count + start + chunk]
+            real_part = row_real * col_real + row_imag * col_imag
+            imag_part = row_imag * col_real - row_real * col_imag
+            first = row * col_count
+            cross_ref[first : first + col_count, start : start + chunk] = real_part.astype(jnp.bfloat16)
+            cross_ref[first : first + col_count, freq_count + start : freq_count + start + chunk] = (
+                imag_part.astype(jnp.bfloat16)
+            )
+    out_ref[...] = jnp.dot(cross_ref[...], table_ref[...], preferred_element_type=jnp.float32)
+
+
 def correlate(row_block, col_block, table):
     hour_count, row_count, part_count, freq_count = row_block.shape
     trace_count = col_block.shape[1]
-    row_step = 4
-    grouped = row_block.reshape(
-        hour_count, row_count // row_step, row_step, part_count, freq_count
-    ).transpose(1, 0, 2, 3, 4)
-
-    def one_block(sub_rows):
-        spectrum = cross_spectrum(sub_rows, col_block)
-        return jnp.einsum("hpk,kl->pl", spectrum, table, preferred_element_type=jnp.float32)
-
-    result = lax.map(one_block, grouped)
-    return result.reshape(row_count * trace_count, table.shape[1])
+    wide = part_count * freq_count
+    rows = row_block.reshape(row_count, wide).astype(jnp.float32)
+    cols = col_block.reshape(trace_count, wide).astype(jnp.float32)
+    lag_count = table.shape[1]
+    row_step = 8
+    return pl.pallas_call(
+        correlate_kernel,
+        grid=(row_count // row_step,),
+        in_specs=[
+            pl.BlockSpec((row_step, wide), lambda i: (i, 0)),
+            pl.BlockSpec((trace_count, wide), lambda i: (0, 0)),
+            pl.BlockSpec((wide, lag_count), lambda i: (0, 0)),
+        ],
+        out_specs=pl.BlockSpec((row_step * trace_count, lag_count), lambda i: (i, 0)),
+        out_shape=jax.ShapeDtypeStruct((row_count * trace_count, lag_count), jnp.float32),
+        scratch_shapes=[pltpu.VMEM((row_step * trace_count, wide), jnp.bfloat16)],
+    )(rows, cols, table)
 
 
 def on_device(spectra, validity):

time: 537 us -> 239 us (0.45)
  other arithmetic: 258 us -> 24.9 us
  local copies, waits for them, and re-layouts: 92.2 us -> 24.5 us
  Pallas kernels: 0 us -> 23.2 us
  matrix products: 17.3 us -> 0 us
    another operation x61 -> x1, other arithmetic: 207 us -> 8.69 us
    while x150 -> x0, local copies, waits for them, and re-layouts: 55.7 us -> none
    convert_element_type x30 -> x3, other arithmetic: 31.7 us -> 3.88 us  [the longest x2 2.21 us: correlate(): rows = row_block.reshape(row_count, wide).astype(jnp.float32)]
    pallas_call x0 -> x3, Pallas kernels: none -> 23.2 us  [correlate(): pl.pallas_call(correlate_kernel, grid=(row_count // row_step,), in_specs=...]
    squeeze x30 -> x0, local copies, waits for them, and re-layouts: 19.1 us -> none  [correlate(): result = lax.map(one_block, grouped)]
    dot_general x30 -> x0, matrix products: 17.3 us -> none  [one_block(): jnp.einsum('hpk,kl->pl', spectrum, table, preferred_element_type=jnp.floa...]
  transfers between devices with their start and end apart: 4 -> 4, of which waited for: 0 -> 1; matrix products, arithmetic and copies ran while one was open for 39% -> 11% of each run, Pallas kernels for 0% -> 4%
where the time goes in v2:
time: 239 us
  blocking collectives  156 us (65%)
  other arithmetic  24.9 us (10%)
  local copies, waits for them, and re-layouts  24.5 us (10%)
  Pallas kernels  23.2 us (10%)
  starting transfers between devices  6.46 us (3%)
  waiting for transfers between devices  2.69 us (1%)
    all_to_all x1, blocking collectives, on_device(): incoming = lax.all_to_all(outgoing, 'hours', 0, 0, tiled=True)  156 us
    pallas_call x3, Pallas kernels, correlate(): pl.pallas_call(correlate_kernel, grid=(row_count // row_step,), in_specs=...  23.2 us
    another operation x1, other arithmetic  8.69 us
    ppermute x4, starting transfers between devices, passed_along(): return lax.ppermute(block, axis, route)  6.46 us
    unnamed x13, local copies, waits for them, and re-layouts  6.1 us
    another operation x2, local copies, waits for them, and re-layouts, on_device(): jnp.stack([correlate(white, panels[round_index][0], table) for round_inde...  5.72 us
    reshape x2, local copies, waits for them, and re-layouts, on_device(): far_slots = far_terms.reshape(hour_devices, share_far, lag_count)  5.3 us
  transfers between devices with their start and end apart: 4, of which 1 were waited for; matrix products, arithmetic and copies ran while one was open for 11% of the time, Pallas kernels for 4%

profile of v2, /device:TPU:1, one launch (start us, length us, event | category | flops | bytes accessed | tf_op | source)
XLA Modules:
  0.0 238.5 jit_solution(701227424341288625)
XLA Ops:
  0.6 0.7 convert_bitcast_fusion
  1.4 2.5 %collective-permute-start.2 = (bf16[1,16]{1,0:T(2,128)(2,1)S(1)}, bf16[1,16]{1,0:T(2,128)(2,1)S(1)}, u32[]{:S(2)}, u32[]{:S(2)}) collective-permute-start(bf16[1,16]{1,0:T(2,128)(2,1)S(1)} %get-tuple-element.11), channel_id=1, source_target_pairs={{3,0},{0,1},{1,2},{2,3},{7,4},{4,5},{5,6},{6,7},{11,8},{8,9},{9,10... | collective-permute-start | bytes 104 | tf_op jit(solution)/shard_map/ppermute | solution.py:20
  3.8 3.0 %collective-permute-start.3 = (bf16[1,16]{1,0:T(2,128)(2,1)S(1)}, bf16[1,16]{1,0:T(2,128)(2,1)S(1)}, u32[]{:S(2)}, u32[]{:S(2)}) collective-permute-start(bf16[1,16]{1,0:T(2,128)(2,1)S(1)} %get-tuple-element.11), channel_id=1, source_target_pairs={{2,0},{3,1},{0,2},{1,3},{6,4},{7,5},{4,6},{5,7},{10,8},{11,9},{8,1... | collective-permute-start | bytes 104 | tf_op jit(solution)/shard_map/ppermute | solution.py:20
  6.8 2.3 multiply_reduce_fusion
  9.1 0.3 reshape.197
  9.4 0.2 reduce_sum.27
  9.7 0.2 mul.136
  9.9 0.1 copy.35
  10.0 1.2 multiply_convert_fusion.2
  11.2 1.0 collective-permute-start
  12.3 0.1 mul.150
  12.4 0.4 mul.138
  12.8 0.5 copy.23
  13.3 0.5 copy.21
  13.8 8.7 %multiply_convert_fusion.1 = (bf16[2048,256]{1,0:T(8,128)(2,1)S(1)}, bf16[2048,256]{1,0:T(8,128)(2,1)S(1)}) fusion(s32[256]{0:T(256)S(1)} %iota_add_fusion), kind=kLoop, calls=%fused_computation.10 | loop fusion | flops 9961472 | bytes 2098176 | tf_op jit(solution)/shard_map/convert.4
  22.4 1.0 fusion.7.rows_ref.cols_ref
  23.4 1.5 pad_maximum_fusion.1.table_ref
  24.9 8.8 %shard_map.41 = f32[2304,256]{1,0:T(8,128)} custom-call(f32[48,4096]{1,0:T(8,128)} %fusion.7.rows_ref.cols_ref, f32[48,4096]{1,0:T(8,128)} %fusion.7.rows_ref.cols_ref, bf16[4096,256]{1,0:T(8,128)(2,1)} %pad_maximum_fusion.1.table_ref), custom_call_target="tpu_custom_call" | custom-call | tf_op jit(solution)/shard_map/pallas_call | solution.py:94
  33.7 2.4 %stack.12 = f32[1,64,36,256]{3,2,1,0:T(8,128)S(1)} reshape(f32[2304,256]{1,0:T(8,128)} %shard_map.41) | data formatting | bytes 4718592 | tf_op jit(solution)/shard_map/stack | solution.py:122
  36.2 0.1 mul.155
  36.4 0.1 select_n.64
  36.6 0.1 reshape.192
  36.8 0.1 mul.162
  36.8 0.1 broadcast_multiply_fusion.1
  36.9 0.1 mul.154
  37.0 0.1 mul.158
  37.1 0.1 reshape.198
  37.3 0.1 fusion.9
  37.3 2.7 %collective-permute-done.1 = bf16[1,48,2,2048]{3,2,1,0:T(2,128)(2,1)} collective-permute-done((bf16[1,48,2,2048]{3,2,1,0:T(2,128)(2,1)}, bf16[1,48,2,2048]{3,2,1,0:T(2,128)(2,1)}, u32[]{:S(2)}, u32[]{:S(2)}) %collective-permute-start.1) | collective-permute-done | bytes 393248 | tf_op jit(solution)/shard_map/ppermute | solution.py:20
  40.0 1.2 fusion.8
  41.2 1.0 copy.25
  42.2 1.7 fusion.6
  43.9 1.4 copy.26
  45.3 2.0 copy.24
  47.3 5.7 %shard_map.43 = f32[1152,256]{1,0:T(8,128)} custom-call(f32[24,4096]{1,0:T(8,128)} %bitcast.54, f32[48,4096]{1,0:T(8,128)} %bitcast.53, bf16[4096,256]{1,0:T(8,128)(2,1)} %pad_maximum_fusion.1.table_ref), custom_call_target="tpu_custom_call" | custom-call | tf_op jit(solution)/shard_map/pallas_call | solution.py:94
  53.0 2.5 %reshape.190 = f32[64,18,256]{2,1,0:T(8,128)} reshape(f32[1152,256]{1,0:T(8,128)} %shard_map.43) | data formatting | bytes 2359296 | tf_op jit(solution)/shard_map/reshape | solution.py:151
  55.5 2.8 %copy.14 = f32[64,18,256]{2,0,1:T(8,128)} copy(f32[64,18,256]{2,1,0:T(8,128)} %reshape.190) | data formatting | bytes 2359296 | tf_op jit(solution)/shard_map/reshape | solution.py:151
  58.3 8.8 %shard_map.42 = f32[2304,256]{1,0:T(8,128)} custom-call(f32[48,4096]{1,0:T(8,128)} %fusion.7.rows_ref.cols_ref, f32[48,4096]{1,0:T(8,128)} %bitcast.52, bf16[4096,256]{1,0:T(8,128)(2,1)} %pad_maximum_fusion.1.table_ref), custom_call_target="tpu_custom_call" | custom-call | tf_op jit(solution)/shard_map/pallas_call | solution.py:94
  67.0 3.3 %stack.13 = f32[1,64,36,256]{3,2,1,0:T(8,128)} reshape(f32[2304,256]{1,0:T(8,128)} %shard_map.42) | data formatting | bytes 4718592 | tf_op jit(solution)/shard_map/stack | solution.py:122
  70.4 2.1 maximum_bitcast_fusion
  72.5 1.4 copy.11
  73.9 0.8 pad_maximum_fusion
  74.6 3.5 %copy.15 = f32[64,91,256]{2,1,0:T(8,128)S(1)} copy(f32[64,91,256]{2,0,1:T(8,128)S(1)} %pad_maximum_fusion) | data formatting | bytes 11927552 | tf_op jit(solution)/shard_map/concatenate | solution.py:161
  78.1 155.8 %all_to_all.5 = f32[64,91,256]{2,1,0:T(8,128)} all-to-all(f32[64,91,256]{2,1,0:T(8,128)S(1)} %copy.15), channel_id=1, replica_groups=mesh['hours'=64,'blocks'=4] {'hours'}, dimensions={0} | all-to-all | bytes 11927552 | tf_op jit(solution)/shard_map/all_to_all | solution.py:164
  233.9 3.2 %reduce_sum.28 = f32[91,256]{1,0:T(8,128)S(1)} reduce(f32[64,91,256]{2,1,0:T(8,128)} %all_to_all.5, f32[]{:T(128)} %constant.13.clone.1), dimensions={0}, to_apply=%region_2.3 | reduce | flops 1467648 | bytes 6056964 | tf_op jit(solution)/shard_map/reduce_sum | solution.py:165
  237.1 0.1 slice_divide_fusion
  237.2 0.6 broadcast_in_dim.29
  237.9 0.7 copy.16
  (28 shorter events, 0.7 us)
Async XLA Ops:
  0.6 9.4 %copy-start = (f32[1,16,3,2,2048]{4,3,2,1,0:T(2,128)S(1)}, f32[1,16,3,2,2048]{4,3,2,1,0:T(2,128)}, u32[]{:S(2)}) copy-start(f32[1,16,3,2,2048]{4,3,2,1,0:T(2,128)} %param.2) | copy-start | bytes 2359300
  1.4 34.7 %collective-permute-start.2 = (bf16[1,16]{1,0:T(2,128)(2,1)S(1)}, bf16[1,16]{1,0:T(2,128)(2,1)S(1)}, u32[]{:S(2)}, u32[]{:S(2)}) collective-permute-start(bf16[1,16]{1,0:T(2,128)(2,1)S(1)} %get-tuple-element.11), channel_id=1, source_target_pairs={{3,0},{0,1},{1,2},{2,3},{7,4},{4,5},{5,6},{6,7},{11,8},{8,9},{9,10... | collective-permute-start | bytes 104 | tf_op jit(solution)/shard_map/ppermute | solution.py:20
  3.8 32.4 %collective-permute-start.3 = (bf16[1,16]{1,0:T(2,128)(2,1)S(1)}, bf16[1,16]{1,0:T(2,128)(2,1)S(1)}, u32[]{:S(2)}, u32[]{:S(2)}) collective-permute-start(bf16[1,16]{1,0:T(2,128)(2,1)S(1)} %get-tuple-element.11), channel_id=1, source_target_pairs={{2,0},{3,1},{0,2},{1,3},{6,4},{7,5},{4,6},{5,7},{10,8},{11,9},{8,1... | collective-permute-start | bytes 104 | tf_op jit(solution)/shard_map/ppermute | solution.py:20
  10.0 3.3 %copy-start.1 = (f32[6,8,16,128]{3,1,2,0:T(8,128)}, f32[6,8,16,128]{3,1,2,0:T(8,128)S(1)}, u32[]{:S(2)}) copy-start(f32[6,8,16,128]{3,1,2,0:T(8,128)S(1)} %copy.35) | copy-start | bytes 1179652
  11.2 28.8 %collective-permute-start.1 = (bf16[1,48,2,2048]{3,2,1,0:T(2,128)(2,1)}, bf16[1,48,2,2048]{3,2,1,0:T(2,128)(2,1)}, u32[]{:S(2)}, u32[]{:S(2)}) collective-permute-start(bf16[1,48,2,2048]{3,2,1,0:T(2,128)(2,1)} %multiply_convert_fusion.2), channel_id=1, source_target_pairs={{2,0},{3,1},{0,2},{1,3},{6,4},{7,5},{4,6},{5,7},{10,8},{11,9},{8,1... | collective-permute-start | bytes 1179656 | tf_op jit(solution)/shard_map/ppermute | solution.py:20
  11.2 34.1 %collective-permute-start = (bf16[1,48,2,2048]{3,2,1,0:T(2,128)(2,1)}, bf16[1,48,2,2048]{3,2,1,0:T(2,128)(2,1)}, u32[]{:S(2)}, u32[]{:S(2)}) collective-permute-start(bf16[1,48,2,2048]{3,2,1,0:T(2,128)(2,1)} %multiply_convert_fusion.2), channel_id=1, source_target_pairs={{3,0},{0,1},{1,2},{2,3},{7,4},{4,5},{5,6},{6,7},{11,8},{8,9},{9,10... | collective-permute-start | bytes 1179656 | tf_op jit(solution)/shard_map/ppermute | solution.py:20
  72.5 1.4 copy-start.2
